TPU v7x, 256 devices: a whole 4x4x8 slice. The times are simulated.
256 devices in a mesh: dp: 8 (over z), seq: 32 (over y, x, core).
Axes of the slice: x: 4, y: 4, z: 8, core: 2. Of those that a mesh axis runs over, the one named last changes fastest.
Arguments:
- inputs: bfloat16 [8, 4096, 2048], P('dp', 'seq'), may hold values from -6 to 6
- weight_codes: bfloat16 [2048, 1280], P('seq'), may hold values from -4 to 4
- scales: bfloat16 [2048, 10], P('seq'), may hold values from 0.010986328 to 0.043945312
- log_decay: float32 [8, 16, 4096], P('dp', None, 'seq'), may hold values from -0.85 to 0, as said below
- cotangent: bfloat16 [8, 4096, 1024], P('dp', 'seq'), may hold values from -6 to 6
Outputs:
- grad_inputs: float32 [8, 4096, 2048], P('dp', 'seq')
- grad_weight: float32 [2048, 1280], P('seq')
Inputs may be any that keep to these rules, and one draw needn't show every extreme that they name: log_decay is negative everywhere.
All inputs are finite; a program needn't handle non-finite values.
Results may differ from a plain program's by a relative error of at most 0.017.
Values may be sent and summed in bfloat16 or wider, within the bound.
No kernel may reach another device: no remote copies, remote signals or barrier semaphores. Data moves between devices by JAX's collectives and lax.ppermute only.
A program may use at most 128 MiB of HBM per device.

v0:
```python
import math
import jax
import jax.numpy as jnp
from jax import lax
from jax.sharding import PartitionSpec as P


def entering(part, axis, combine, identity, reverse):
    count = lax.axis_size(axis)
    place = lax.axis_index(axis)
    ahead = count - 1 - place if reverse else place
    gathered = jax.tree.map(lambda a: lax.all_gather(a, axis), part)
    state = jax.tree.map(lambda a, e: jnp.zeros_like(a) + jnp.asarray(e, a.dtype), part, identity)

    def one(hop, state):
        source = count - 1 - hop if reverse else hop
        return combine(
            state, jax.tree.map(lambda a: lax.dynamic_index_in_dim(a, source, 0, False), gathered)
        )

    return lax.fori_loop(0, ahead, one, state)


def dequantize(code_rows, scale_rows):
    row_count, col_count = code_rows.shape
    group_count = scale_rows.shape[1]
    spread = code_rows.astype(jnp.float32).reshape(row_count, group_count, col_count // group_count)
    spread = spread * scale_rows.astype(jnp.float32)[:, :, None]
    return spread.reshape(row_count, col_count).astype(jnp.bfloat16)


def block_prep(ld_block):
    cum_log = jnp.cumsum(ld_block, axis=1)
    input_scale = jnp.sqrt(-jnp.expm1(2.0 * ld_block))
    tail_weight = jnp.exp(cum_log[:, -1:] - cum_log) * input_scale
    return (cum_log, input_scale, tail_weight)


def weighted_pair(x_vals, grad_out, tail_weight, cum_log, inv_root):
    head_weight = jnp.exp(cum_log) * inv_root
    weighted_x = (x_vals.astype(jnp.float32) * tail_weight.T[:, :, None]).astype(jnp.bfloat16)
    weighted_g = (grad_out.astype(jnp.float32) * head_weight.T[:, :, None]).astype(jnp.bfloat16)
    return (weighted_x, weighted_g)


def summaries(x_vals, b_mat, c_mat, grad_out, ld_block):
    cum_log, input_scale, tail_weight = block_prep(ld_block)
    inv_root = 1.0 / math.sqrt(b_mat.shape[1])
    weighted_x, weighted_g = weighted_pair(x_vals, grad_out, tail_weight, cum_log, inv_root)
    fwd_state = jnp.einsum("sn,shp->hnp", b_mat, weighted_x, preferred_element_type=jnp.float32)
    back_state = jnp.einsum("tn,thp->hnp", c_mat, weighted_g, preferred_element_type=jnp.float32)
    return (jnp.exp(cum_log[:, -1]), fwd_state, back_state)


def block_grads(x_vals, b_mat, c_mat, grad_out, ld_block, state_in, back_in):
    block_len = ld_block.shape[1]
    cum_log, input_scale, tail_weight = block_prep(ld_block)
    inv_root = 1.0 / math.sqrt(b_mat.shape[1])
    weighted_x, weighted_g = weighted_pair(x_vals, grad_out, tail_weight, cum_log, inv_root)
    row_ids = lax.broadcasted_iota(jnp.int32, (block_len, block_len), 0)
    col_ids = lax.broadcasted_iota(jnp.int32, (block_len, block_len), 1)
    lower_mask = (row_ids >= col_ids)[None]
    log_gap = cum_log[:, :, None] - cum_log[:, None, :]
    decay_mat = jnp.where(lower_mask, jnp.exp(jnp.where(lower_mask, log_gap, 0.0)), 0.0)
    state_low = state_in.astype(jnp.bfloat16)
    back_low = back_in.astype(jnp.bfloat16)
    x_dot_g = jnp.einsum("thp,shp->hts", grad_out, x_vals, preferred_element_type=jnp.float32)
    c_dot_b = jnp.dot(c_mat, b_mat.T, preferred_element_type=jnp.float32)
    mix_weights = (
        jnp.sum(decay_mat * input_scale[:, None, :] * x_dot_g, axis=0) * inv_root
    ).astype(jnp.bfloat16)
    d_c = jnp.einsum("hnp,thp->tn", state_low, weighted_g, preferred_element_type=jnp.float32)
    d_c = d_c + jnp.dot(mix_weights, b_mat, preferred_element_type=jnp.float32)
    d_b = jnp.einsum("hnp,thp->tn", back_low, weighted_x, preferred_element_type=jnp.float32)
    d_b = d_b + jnp.dot(mix_weights.T, c_mat, preferred_element_type=jnp.float32)
    d_x = (
        jnp.einsum("tn,hnp->thp", b_mat, back_low, preferred_element_type=jnp.float32)
        * tail_weight.T[:, :, None]
    )
    inner_weights = (decay_mat * c_dot_b[None] * inv_root).astype(jnp.bfloat16)
    inner = jnp.einsum("hus,uhp->shp", inner_weights, grad_out, preferred_element_type=jnp.float32)
    d_x = d_x + input_scale.T[:, :, None] * inner
    return (d_x, d_b, d_c)


def state_chain(decays, adds, start, backward):

    def step(carry, item):
        return (item[0][:, None, None] * carry + item[1], carry)

    return lax.scan(step, start, (decays, adds), reverse=backward)


def join_summary(earlier, later):
    return (earlier[0] * later[0], later[0][:, None, None] * earlier[1] + later[1])


def local(inputs, weight_codes, scales, log_decay, cotangent):
    tok_count = inputs.shape[1]
    features = inputs[0]
    grad_out = cotangent[0]
    head_count = log_decay.shape[1]
    hp_width = grad_out.shape[1]
    head_dim = hp_width // head_count
    proj_width = weight_codes.shape[1]
    state_width = (proj_width - hp_width) // 2
    full_codes, full_scales = (
        lax.all_gather(weight_codes, "seq", axis=0, tiled=True),
        lax.all_gather(scales, "seq", axis=0, tiled=True),
    )
    weights = dequantize(full_codes, full_scales)
    projected = jnp.dot(features, weights, preferred_element_type=jnp.float32).astype(jnp.bfloat16)
    block_len = min(128, tok_count)
    block_count = tok_count // block_len
    x_blocks = projected[:, :hp_width].reshape(block_count, block_len, head_count, head_dim)
    b_blocks = projected[:, hp_width : hp_width + state_width].reshape(
        block_count, block_len, state_width
    )
    c_blocks = projected[:, hp_width + state_width :].reshape(block_count, block_len, state_width)
    g_blocks = grad_out.reshape(block_count, block_len, head_count, head_dim)
    ld_blocks = log_decay[0].reshape(head_count, block_count, block_len).transpose(1, 0, 2)
    decays, fwd_states, back_states = jax.vmap(summaries)(
        x_blocks, b_blocks, c_blocks, g_blocks, ld_blocks
    )
    zero_state = jnp.zeros((head_count, state_width, head_dim), jnp.float32)
    dev_decay = jnp.prod(decays, axis=0)
    dev_fwd, unused_a = state_chain(decays, fwd_states, zero_state, False)
    dev_back, unused_b = state_chain(decays, back_states, zero_state, True)
    neutral = (jnp.ones((head_count,), jnp.float32), zero_state)
    carried = entering((dev_decay, dev_fwd), "seq", join_summary, neutral, False)
    returned = entering((dev_decay, dev_back), "seq", join_summary, neutral, True)
    unused_c, state_starts = state_chain(decays, fwd_states, carried[1], False)
    unused_d, back_starts = state_chain(decays, back_states, returned[1], True)
    d_x, d_b, d_c = lax.map(
        lambda block_item: block_grads(*block_item),
        (x_blocks, b_blocks, c_blocks, g_blocks, ld_blocks, state_starts, back_starts),
    )
    d_proj = jnp.concatenate(
        [
            d_x.reshape(tok_count, hp_width),
            d_b.reshape(tok_count, state_width),
            d_c.reshape(tok_count, state_width),
        ],
        axis=1,
    ).astype(jnp.bfloat16)
    grad_in = lax.dot_general(
        d_proj, weights, (((1,), (1,)), ((), ())), preferred_element_type=jnp.float32
    )
    seq_count = lax.axis_size("seq")
    group_count = lax.axis_size("dp")
    norm_factor = 1.0 / math.sqrt(group_count * seq_count * tok_count)
    partial_grad = lax.psum_scatter(
        lax.dot_general(
            features, d_proj, (((0,), (0,)), ((), ())), preferred_element_type=jnp.float32
        ),
        "seq",
        scatter_dimension=0,
        tiled=True,
    )
    summed_grad = lax.psum(partial_grad, "dp")
    return (grad_in[None], summed_grad * norm_factor)


def solution(mesh):
    placed = (
        P("dp", "seq", None),
        P("seq", None),
        P("seq", None),
        P("dp", None, "seq"),
        P("dp", "seq", None),
    )
    return jax.shard_map(
        local,
        mesh=mesh,
        in_specs=placed,
        out_specs=(P("dp", "seq", None), P("seq", None)),
        check_vma=False,
    )
```

profile of v0, /device:TPU:2, one launch (start us, length us, event | category | flops | bytes accessed | tf_op | source)
XLA Modules:
  0.0 521.6 jit_solution(17085878530613788069)
XLA Ops:
  8.0 24.6 %all-gather.1 = bf16[32,64,10]{1,2,0:T(8,128)(2,1)S(1)} all-gather(bf16[1,64,10]{1,2,0:T(8,128)(2,1)} %bitcast.145), channel_id=1, replica_groups=mesh['dp'=8,'seq'=32] {'seq'}, dimensions={0}, use_global_device_ids=true | all-gather | bytes 42240 | tf_op jit(solution)/shard_map/all_gather | solution.py:109
  32.7 1.0 reduce_window_sum.23
  33.8 1.0 reduce_window_sum.24
  35.0 0.8 multiply_bitcast_fusion.3
  35.8 1.3 fusion.43
  37.1 28.6 %all-gather.6.cloned.1.call-done = bf16[2048,1280]{1,0:T(8,128)(2,1)} async-done(((bf16[64,1280]{1,0:T(8,128)(2,1)}), bf16[2048,1280]{1,0:T(8,128)(2,1)}) %all-gather.6.cloned.1.call-update) | async-done | bytes 5242896 | tf_op jit(solution)/shard_map/all_gather | solution.py:108
  65.7 7.9 %copy.59 = bf16[2048,1280]{0,1:T(8,128)(2,1)} copy(bf16[2048,1280]{1,0:T(8,128)(2,1)} %all-gather.6.cloned.1.call-done) | data formatting | bytes 10485760 | tf_op jit(solution)/shard_map/all_gather | solution.py:108
  73.6 3.9 fusion
  77.6 2.4 copy-done.2
  80.0 1.5 fusion.1
  81.5 0.8 fusion.15
  82.3 1.0 fusion.9
  83.6 0.8 fusion.13
  84.4 1.0 fusion.7
  85.5 21.4 %all-gather = f32[32,16,1]{1,2,0:T(1,128)} all-gather(f32[1,16,1]{1,2,0:T(1,128)S(1)} %exp.58), channel_id=2, replica_groups=mesh['dp'=8,'seq'=32] {'seq'}, dimensions={0}, use_global_device_ids=true | all-gather | bytes 2112 | tf_op jit(solution)/shard_map/all_gather | solution.py:12
  106.9 0.9 fusion.3
  107.8 0.8 fusion.29
  108.7 52.1 %all-gather.10.cloned.1.call-done = f32[32,16,128,64]{2,3,1,0:T(8,128)} async-done(((f32[1,16,128,64]{2,3,1,0:T(8,128)}), f32[32,16,128,64]{2,3,1,0:T(8,128)}) %all-gather.10.cloned.1.call-update) | async-done | bytes 16777232 | tf_op jit(solution)/shard_map/all_gather | solution.py:12
  160.9 4.7 while.17
  160.9 1.1 constant_dynamic-slice_fusion.5
  163.3 1.1 constant_dynamic-slice_fusion.5
  165.6 74.8 %all-gather.8.cloned.1.call-done = f32[32,16,128,64]{2,3,1,0:T(8,128)} async-done(((f32[1,16,128,64]{2,3,1,0:T(8,128)}), f32[32,16,128,64]{2,3,1,0:T(8,128)}) %all-gather.8.cloned.1.call-update) | async-done | bytes 16777232 | tf_op jit(solution)/shard_map/all_gather | solution.py:12
  240.5 68.7 %while.16 = (s32[]{:T(128)}, f32[16,128,64]{2,1,0:T(8,128)S(1)}, s32[]{:T(128)}, f32[32,16]{1,0:T(8,128)}, f32[32,16,128,64]{2,3,1,0:T(8,128)}, /*index=5*/s32[]{:T(128)}, s32[]{:T(128)}, s32[]{:T(128)}, s32[]{:T(128)}) while((s32[]{:T(128)}, f32[16,128,64]{2,1,0:T(8,128)S(1)}, s32[]{:T(128)}, f32[32,16]{1,0:T(8,128)}, ...), condition=%wide.region_2.3_spmd, body=%wide.region_1.2_spmd.sunk | while | flops 262150 | bytes 3670363 | solution.py:21
  240.6 1.1 constant_dynamic-slice_fusion.4
  242.0 0.7 dynamic-slice_bitcast_fusion.4
  242.9 1.1 constant_dynamic-slice_fusion.4
  245.3 1.1 constant_dynamic-slice_fusion.4
  247.7 1.1 constant_dynamic-slice_fusion.4
  250.1 1.1 constant_dynamic-slice_fusion.4
  252.4 1.1 constant_dynamic-slice_fusion.4
  253.9 0.7 dynamic-slice_bitcast_fusion.4
  254.8 1.1 constant_dynamic-slice_fusion.4
  257.2 1.1 constant_dynamic-slice_fusion.4
  259.5 1.1 constant_dynamic-slice_fusion.4
  261.9 1.1 constant_dynamic-slice_fusion.4
  264.3 1.1 constant_dynamic-slice_fusion.4
  266.6 1.1 constant_dynamic-slice_fusion.4
  269.0 1.1 constant_dynamic-slice_fusion.4
  271.4 1.1 constant_dynamic-slice_fusion.4
  273.7 1.1 constant_dynamic-slice_fusion.4
  276.1 1.1 constant_dynamic-slice_fusion.4
  278.4 1.1 constant_dynamic-slice_fusion.4
  280.8 1.1 constant_dynamic-slice_fusion.4
  283.2 1.1 constant_dynamic-slice_fusion.4
  285.6 1.1 constant_dynamic-slice_fusion.4
  287.9 1.1 constant_dynamic-slice_fusion.4
  290.3 1.1 constant_dynamic-slice_fusion.4
  292.7 1.1 constant_dynamic-slice_fusion.4
  295.0 1.1 constant_dynamic-slice_fusion.4
  297.4 1.1 constant_dynamic-slice_fusion.4
  299.8 1.1 constant_dynamic-slice_fusion.4
  302.1 1.1 constant_dynamic-slice_fusion.4
  304.5 1.1 constant_dynamic-slice_fusion.4
  306.9 1.1 constant_dynamic-slice_fusion.4
  309.6 1.2 convolution_bitcast_fusion.7
  310.8 1.5 convolution_bitcast_fusion.6
  313.5 5.3 %convolution_bitcast_fusion = f32[2048,1280]{0,1:T(8,128)} fusion(bf16[1,128,2048]{2,1,0:T(8,128)(2,1)S(1)} %copy-done, bf16[128,128]{0,1:T(8,128)(2,1)S(1)} %fusion.12, bf16[128,128]{0,1:T(8,128)(2,1)S(1)} %fusion.11, bf16[128,1024]{0,1:T(8,128)(2,1)S(1)} %bitcast.132), kind=kOutput, calls=%fused_computation.8 | convolution fusion | flops 672071680 | bytes 11337728 | tf_op jit(solution)/shard_map/dot_general | solution.py:153
  318.9 11.3 %copy.89 = f32[2048,1280]{1,0:T(8,128)} copy(f32[2048,1280]{0,1:T(8,128)} %convolution_bitcast_fusion) | data formatting | bytes 20971520
  330.2 106.7 %reduce-scatter.4.cloned.1.call-done = f32[64,1280]{1,0:T(8,128)} async-done(((f32[2048,1280]{1,0:T(8,128)}), f32[64,1280]{1,0:T(8,128)}) %reduce-scatter.4.cloned.1.call-update) | async-done | bytes 327696
  436.9 2.1 copy.90
  439.0 4.3 convolution_bitcast_fusion.1
  443.4 69.7 %all-reduce.2.cloned.1.call-done = f32[64,1280]{0,1:T(8,128)} async-done(((f32[64,1280]{0,1:T(8,128)}), f32[64,1280]{0,1:T(8,128)}) %all-reduce.2.cloned.1.call-update) | async-done | bytes 327696 | tf_op jit(solution)/shard_map/psum | solution.py:160
  513.0 1.1 broadcast_multiply_fusion
  514.2 0.9 copy.77
  (138 shorter events, 40.5 us)
Async XLA Ops:
  7.2 72.8 %copy-start = (bf16[1,128,2048]{2,1,0:T(8,128)(2,1)S(1)}, bf16[1,128,2048]{2,1,0:T(8,128)(2,1)}, u32[]{:S(2)}) copy-start(bf16[1,128,2048]{2,1,0:T(8,128)(2,1)} %param.9) | copy-start | bytes 1572868
  7.2 58.5 %all-gather.6.cloned.1.call-start = ((), (), s32[]{:S(2)}) async-start(), calls=%async_computation.1 | async-start | bytes 5406720 | tf_op jit(solution)/shard_map/all_gather | solution.py:108
  7.9 152.9 %all-gather.10.cloned.1.call-start = ((), (), s32[]{:S(2)}) async-start(), calls=%async_computation.3 | async-start | bytes 17301504 | tf_op jit(solution)/shard_map/all_gather | solution.py:12
  77.6 2.4 copy-start.2
  79.9 3.4 copy-start.5
  83.3 157.1 %all-gather.8.cloned.1.call-start = ((), (), s32[]{:S(2)}) async-start(), calls=%async_computation.2 | async-start | bytes 17301504 | tf_op jit(solution)/shard_map/all_gather | solution.py:12
  83.6 77.2 %copy-start.3 = (bf16[1,128,1024]{1,2,0:T(8,128)(2,1)}, bf16[1,128,1024]{1,2,0:T(8,128)(2,1)S(1)}, u32[]{:S(2)}) copy-start(bf16[1,128,1024]{1,2,0:T(8,128)(2,1)S(1)} %copy.63) | copy-start | bytes 786436
  85.4 351.5 %reduce-scatter.4.cloned.1.call-start = ((), (), s32[]{:S(2)}) async-start(), calls=%async_computation.5 | async-start | bytes 10813440
  106.9 53.9 %copy-start.7 = (pred[128,128]{0,1:T(8,128)(4,1)}, pred[128,128]{0,1:T(8,128)(4,1)S(1)}, u32[]{:S(2)}) copy-start(pred[128,128]{0,1:T(8,128)(4,1)S(1)} %iota_compare_fusion) | copy-start | bytes 49156
  165.6 74.9 %copy-start.1 = (f32[16,128,64]{2,1,0:T(8,128)}, f32[16,128,64]{2,1,0:T(8,128)S(1)}, u32[]{:S(2)}) copy-start(f32[16,128,64]{2,1,0:T(8,128)S(1)} %get-tuple-element.218) | copy-start | bytes 1572868
  309.2 3.7 copy-start.4
  309.2 3.7 copy-start.6
  309.2 3.7 copy-start.8
  309.3 3.7 copy-start.9
  330.2 182.8 %all-reduce.2.cloned.1.call-start = ((), (), s32[]{:S(2)}) async-start(), calls=%async_computation.4 | async-start | bytes 1310720 | tf_op jit(solution)/shard_map/psum | solution.py:160
Sparse Core Ops, SparseCore 0:
  10.6 55.0 all-gather.5
  83.4 77.2 all-gather.9
  163.3 77.0 all-gather.7
  330.3 106.5 reduce-scatter.3
  439.2 73.7 all-reduce.1
where the time goes:
time: 525 us; the launch traced here: 522 us
  waiting for transfers between devices  333 us (63%)
  local copies, waits for them, and re-layouts  91.1 us (17%)
  blocking collectives  46 us (9%)
  matrix products  18.9 us (4%)
  other arithmetic  17.6 us (3%)
  between operations  14 us (3%)
    all_gather x2, waiting for transfers between devices, entering(): gathered = jax.tree.map(lambda a: lax.all_gather(a, axis), part)  127 us
    unnamed x6, waiting for transfers between devices  107 us
    psum x1, waiting for transfers between devices, local(): summed_grad = lax.psum(partial_grad, 'dp')  69.7 us
    dynamic_slice x62, local copies, waits for them, and re-layouts, one(): lax.dynamic_index_in_dim(a, source, 0, False)  43.9 us
    all_gather x1, waiting for transfers between devices, local(): lax.all_gather(weight_codes, 'seq', axis=0, tiled=True)  28.6 us
    all_gather x1, blocking collectives, local(): lax.all_gather(scales, 'seq', axis=0, tiled=True)  24.6 us
    mul x31, local copies, waits for them, and re-layouts, join_summary(): later[0][:, None, None] * earlier[1] + later[1]  21.4 us
    all_gather x1, blocking collectives, entering(): gathered = jax.tree.map(lambda a: lax.all_gather(a, axis), part)  21.4 us
  transfers between devices with their start and end apart: 5, of which 5 were waited for; matrix products, arithmetic and copies ran while one was open for 3% of the time, Pallas kernels for 0%

commit v1 on v0

--- a/solution.py
+++ b/solution.py
@@ -157,7 +157,8 @@
         scatter_dimension=0,
         tiled=True,
     )
-    summed_grad = lax.psum(partial_grad, "dp")
+    known = lax.all_gather(partial_grad, axis_name="dp")
+    summed_grad = jnp.sum(known, axis=0)
     return (grad_in[None], summed_grad * norm_factor)
 
 

time: 525 us -> 563 us (1.072)
  other arithmetic: 17.6 us -> 82.5 us
  waiting for transfers between devices: 333 us -> 307 us
    reduce_scatter x0 -> x1, waiting for transfers between devices: none -> 111 us  [local(): lax.psum_scatter(lax.dot_general(features, d_proj, (((0,), (0,)), ((), ()...]
    unnamed x6 -> x5, waiting for transfers between devices: 107 us -> 0.75 us
    psum x1 -> x0, waiting for transfers between devices: 69.7 us -> none  [local(): summed_grad = lax.psum(partial_grad, 'dp')]
    add x31, other arithmetic: 6.79 us -> 68.9 us  [join_summary(): later[0][:, None, None] * earlier[1] + later[1]]
    all_gather x0 -> x1, waiting for transfers between devices: none -> 39.4 us  [local(): known = lax.all_gather(partial_grad, axis_name='dp')]
    unnamed x25 -> x15, local copies, waits for them, and re-layouts: 17 us -> 13.9 us
where the time goes in v1:
time: 563 us; the launch traced here: 558 us
  waiting for transfers between devices  307 us (55%)
  local copies, waits for them, and re-layouts  88.8 us (16%)
  other arithmetic  82.5 us (15%)
  blocking collectives  45.7 us (8%)
  matrix products  19.4 us (3%)
  between operations  14 us (2%)
    all_gather x2, waiting for transfers between devices, entering(): gathered = jax.tree.map(lambda a: lax.all_gather(a, axis), part)  127 us
    reduce_scatter x1, waiting for transfers between devices, local(): lax.psum_scatter(lax.dot_general(features, d_proj, (((0,), (0,)), ((), ()...  111 us
    add x31, other arithmetic, join_summary(): later[0][:, None, None] * earlier[1] + later[1]  68.9 us
    dynamic_slice x62, local copies, waits for them, and re-layouts, one(): lax.dynamic_index_in_dim(a, source, 0, False)  43.8 us
    all_gather x1, waiting for transfers between devices, local(): known = lax.all_gather(partial_grad, axis_name='dp')  39.4 us
    all_gather x1, waiting for transfers between devices, local(): lax.all_gather(weight_codes, 'seq', axis=0, tiled=True)  28.6 us
    all_gather x1, blocking collectives, local(): lax.all_gather(scales, 'seq', axis=0, tiled=True)  24.6 us
    mul x31, local copies, waits for them, and re-layouts, join_summary(): later[0][:, None, None] * earlier[1] + later[1]  21.4 us
  transfers between devices with their start and end apart: 5, of which 5 were waited for; matrix products, arithmetic and copies ran while one was open for 3% of the time, Pallas kernels for 0%

profile of v1, /device:TPU:2, one launch (start us, length us, event | category | flops | bytes accessed | tf_op | source)
XLA Modules:
  0.0 557.9 jit_solution(12936653987714417815)
XLA Ops:
  8.0 24.6 %all-gather.2 = bf16[32,64,10]{1,2,0:T(8,128)(2,1)S(1)} all-gather(bf16[1,64,10]{1,2,0:T(8,128)(2,1)} %bitcast.147), channel_id=1, replica_groups=mesh['dp'=8,'seq'=32] {'seq'}, dimensions={0}, use_global_device_ids=true | all-gather | bytes 42240 | tf_op jit(solution)/shard_map/all_gather | solution.py:109
  35.8 1.3 fusion.43
  37.1 28.6 %all-gather.8.cloned.1.call-done = bf16[2048,1280]{1,0:T(8,128)(2,1)} async-done(((bf16[64,1280]{1,0:T(8,128)(2,1)}), bf16[2048,1280]{1,0:T(8,128)(2,1)}) %all-gather.8.cloned.1.call-update) | async-done | bytes 5242896 | tf_op jit(solution)/shard_map/all_gather | solution.py:108
  65.7 8.0 %copy.58 = bf16[2048,1280]{0,1:T(8,128)(2,1)} copy(bf16[2048,1280]{1,0:T(8,128)(2,1)} %all-gather.8.cloned.1.call-done) | data formatting | bytes 10485760 | tf_op jit(solution)/shard_map/all_gather | solution.py:108
  73.6 3.9 fusion
  77.6 2.4 copy-done.1
  79.9 1.5 fusion.1
  85.5 21.1 %all-gather = f32[32,16,1]{1,2,0:T(1,128)} all-gather(f32[1,16,1]{1,2,0:T(1,128)S(1)} %exp.58), channel_id=2, replica_groups=mesh['dp'=8,'seq'=32] {'seq'}, dimensions={0}, use_global_device_ids=true | all-gather | bytes 2112 | tf_op jit(solution)/shard_map/all_gather | solution.py:12
  108.4 52.5 %all-gather.12.cloned.1.call-done = f32[32,16,128,64]{2,3,1,0:T(8,128)} async-done(((f32[1,16,128,64]{2,3,1,0:T(8,128)}), f32[32,16,128,64]{2,3,1,0:T(8,128)}) %all-gather.12.cloned.1.call-update) | async-done | bytes 16777232 | tf_op jit(solution)/shard_map/all_gather | solution.py:12
  161.0 4.7 while.17
  161.0 1.1 constant_dynamic-slice_fusion.5
  163.3 1.1 constant_dynamic-slice_fusion.5
  165.7 74.8 %all-gather.10.cloned.1.call-done = f32[32,16,128,64]{2,3,1,0:T(8,128)} async-done(((f32[1,16,128,64]{2,3,1,0:T(8,128)}), f32[32,16,128,64]{2,3,1,0:T(8,128)}) %all-gather.10.cloned.1.call-update) | async-done | bytes 16777232 | tf_op jit(solution)/shard_map/all_gather | solution.py:12
  240.5 1.1 broadcast_in_dim.76.clone.1
  241.6 129.8 %while.16 = (s32[]{:T(128)}, f32[16,128,64]{2,1,0:T(8,128)}, s32[]{:T(128)}, f32[32,16]{1,0:T(8,128)}, f32[32,16,128,64]{2,3,1,0:T(8,128)}, /*index=5*/s32[]{:T(128)}, s32[]{:T(128)}, s32[]{:T(128)}, s32[]{:T(128)}) while((s32[]{:T(128)}, f32[16,128,64]{2,1,0:T(8,128)}, s32[]{:T(128)}, f32[32,16]{1,0:T(8,128)}, f32[32,16,128,64]{2,3,1,0:T(8,128)}, ...), condition=%wide.region_2.3_spmd, body=%wide.region_1.2_spmd.sunk | while | flops 262150 | bytes 3670363 | solution.py:21
  241.6 1.1 constant_dynamic-slice_fusion.4
  243.7 2.4 bitcast_add_fusion.4
  246.1 1.1 constant_dynamic-slice_fusion.4
  248.2 2.4 bitcast_add_fusion.4
  250.5 1.1 constant_dynamic-slice_fusion.4
  252.7 2.4 bitcast_add_fusion.4
  255.0 1.1 constant_dynamic-slice_fusion.4
  257.1 2.4 bitcast_add_fusion.4
  261.6 2.4 bitcast_add_fusion.4
  266.1 2.4 bitcast_add_fusion.4
  268.5 1.1 constant_dynamic-slice_fusion.4
  270.6 2.4 bitcast_add_fusion.4
  275.1 2.4 bitcast_add_fusion.4
  279.5 2.4 bitcast_add_fusion.4
  284.0 2.4 bitcast_add_fusion.4
  288.5 2.4 bitcast_add_fusion.4
  293.0 2.4 bitcast_add_fusion.4
  297.5 2.4 bitcast_add_fusion.4
  302.0 2.4 bitcast_add_fusion.4
  306.4 2.4 bitcast_add_fusion.4
  310.9 2.4 bitcast_add_fusion.4
  315.4 2.4 bitcast_add_fusion.4
  317.7 1.1 constant_dynamic-slice_fusion.4
  319.8 2.4 bitcast_add_fusion.4
  324.3 2.4 bitcast_add_fusion.4
  328.8 2.4 bitcast_add_fusion.4
  331.1 1.1 constant_dynamic-slice_fusion.4
  333.2 2.4 bitcast_add_fusion.4
  337.7 2.4 bitcast_add_fusion.4
  342.1 2.4 bitcast_add_fusion.4
  344.5 1.1 constant_dynamic-slice_fusion.4
  346.6 2.4 bitcast_add_fusion.4
  351.1 2.4 bitcast_add_fusion.4
  355.5 2.4 bitcast_add_fusion.4
  360.0 2.4 bitcast_add_fusion.4
  362.4 1.1 constant_dynamic-slice_fusion.4
  364.5 2.4 bitcast_add_fusion.4
  366.9 1.1 constant_dynamic-slice_fusion.4
  369.0 2.4 bitcast_add_fusion.4
  371.3 1.4 convert_element_type.94
  372.9 1.2 convolution_bitcast_fusion.7
  374.2 1.2 convolution_bitcast_fusion.6
  375.9 1.4 fusion.10
  377.4 5.3 convolution_bitcast_fusion
  382.7 11.3 %copy.88 = f32[2048,1280]{1,0:T(8,128)} copy(f32[2048,1280]{0,1:T(8,128)} %convolution_bitcast_fusion) | data formatting | bytes 20971520
  394.1 110.9 %reduce-scatter.4.cloned.1.call-done = f32[64,1280]{1,0:T(8,128)} async-done(((f32[2048,1280]{1,0:T(8,128)}), f32[64,1280]{1,0:T(8,128)}) %reduce-scatter.4.cloned.1.call-update) | async-done | bytes 327696 | tf_op jit(solution)/shard_map/reduce_scatter | solution.py:152
  505.0 4.3 convolution_bitcast_fusion.1
  509.4 39.4 %all-gather.14.cloned.1.call-done = f32[512,1280]{1,0:T(8,128)} async-done(((f32[64,1280]{1,0:T(8,128)}), f32[512,1280]{1,0:T(8,128)}) %all-gather.14.cloned.1.call-update) | async-done | bytes 2621456 | tf_op jit(solution)/shard_map/all_gather | solution.py:160
  548.7 1.9 reduce_sum.20
  (129 shorter events, 64.0 us)
Async XLA Ops:
  7.2 72.8 %copy-start = (bf16[1,128,2048]{2,1,0:T(8,128)(2,1)S(1)}, bf16[1,128,2048]{2,1,0:T(8,128)(2,1)}, u32[]{:S(2)}) copy-start(bf16[1,128,2048]{2,1,0:T(8,128)(2,1)} %param.9) | copy-start | bytes 1572868
  7.2 58.5 %all-gather.8.cloned.1.call-start = ((), (), s32[]{:S(2)}) async-start(), calls=%async_computation.1 | async-start | bytes 5406720 | tf_op jit(solution)/shard_map/all_gather | solution.py:108
  7.9 152.9 %all-gather.12.cloned.1.call-start = ((), (), s32[]{:S(2)}) async-start(), calls=%async_computation.3 | async-start | bytes 17301504 | tf_op jit(solution)/shard_map/all_gather | solution.py:12
  77.6 2.4 copy-start.1
  79.9 3.4 copy-start.4
  83.3 157.2 %all-gather.10.cloned.1.call-start = ((), (), s32[]{:S(2)}) async-start(), calls=%async_computation.2 | async-start | bytes 17301504 | tf_op jit(solution)/shard_map/all_gather | solution.py:12
  83.6 77.3 %copy-start.2 = (bf16[1,128,1024]{1,2,0:T(8,128)(2,1)}, bf16[1,128,1024]{1,2,0:T(8,128)(2,1)S(1)}, u32[]{:S(2)}) copy-start(bf16[1,128,1024]{1,2,0:T(8,128)(2,1)S(1)} %copy.62) | copy-start | bytes 786436
  85.4 419.6 %reduce-scatter.4.cloned.1.call-start = ((), (), s32[]{:S(2)}) async-start(), calls=%async_computation.5 | async-start | bytes 10813440 | tf_op jit(solution)/shard_map/reduce_scatter | solution.py:152
  106.6 54.3 %copy-start.5 = (pred[128,128]{0,1:T(8,128)(4,1)}, pred[128,128]{0,1:T(8,128)(4,1)S(1)}, u32[]{:S(2)}) copy-start(pred[128,128]{0,1:T(8,128)(4,1)S(1)} %iota_compare_fusion) | copy-start | bytes 49156
  371.3 4.6 copy-start.3
  394.0 154.7 %all-gather.14.cloned.1.call-start = ((), (), s32[]{:S(2)}) async-start(), calls=%async_computation.4 | async-start | bytes 2949120 | tf_op jit(solution)/shard_map/all_gather | solution.py:160
Sparse Core Ops, SparseCore 0:
  10.6 55.0 all-gather.7
  83.4 77.3 all-gather.11
  163.4 77.0 all-gather.9
  394.1 110.8 reduce-scatter.3
  506.8 41.9 all-gather.13
